TPU v7x, 32 devices: a whole 2x2x4 slice. The times are simulated.
32 devices in a mesh: req: 2 (over x), ctx: 8 (over z, core), exp: 2 (over y).
Axes of the slice: x: 2, y: 2, z: 4, core: 2. Of those that a mesh axis runs over, the one named last changes fastest.
Arguments:
- query_states: bfloat16 [2, 512, 1024], P('req', 'ctx', 'exp'), may hold values from -6 to 6
- key_states: bfloat16 [2, 512, 1024], P('req', 'ctx', 'exp'), may hold values from -6 to 6
- value_states: bfloat16 [2, 512, 1024], P('req', 'ctx', 'exp'), may hold values from -6 to 6
- residual: bfloat16 [2, 512, 2048], P('req', ('ctx', 'exp')), may hold values from -6 to 6
- out_weight: bfloat16 [2048, 1024], P('ctx', 'exp'), may hold values from -0.1875 to 0.1875
- norm_gain: float32 [2048], replicated, may hold values from 0.1 to 1.9
- gate_weight: bfloat16 [8, 2048, 704], P('ctx', None, 'exp'), may hold values from -0.125 to 0.125
- up_weight: bfloat16 [8, 2048, 704], P('ctx', None, 'exp'), may hold values from -0.125 to 0.125
- down_weight: bfloat16 [8, 704, 2048], P('ctx', 'exp'), may hold values from -0.21875 to 0.21875
- routes: int32 [2, 512, 4], P('req', 'ctx'), may hold values from 0 to 7, all different within a row; in each aligned block of 64 rows (0 to 63, 64 to 127, ..., all dimensions but the last counted through in order) at most 48 rows name the same one
- route_weights: float32 [2, 512, 4], P('req', 'ctx'), may hold values from 0.1 to 1
- prompt_lengths: int32 [2], P('req'), may hold values from 128 to 512, as said below
Outputs:
- layer_out: bfloat16 [2, 512, 2048], P('req', ('ctx', 'exp'))
- cache_keys: bfloat16 [2, 512, 1024], P('req', 'ctx', 'exp')
- cache_values: bfloat16 [2, 512, 1024], P('req', 'ctx', 'exp')
Inputs may be any that keep to these rules, and one draw needn't show every extreme that they name: `routes`: each row names 4 different experts; in each aligned block of 64 rows of a request no expert is named by more than 48 rows, a bound that some block reaches. `prompt_lengths`: one request has exactly 512 tokens.
All inputs are finite; a program needn't handle non-finite values.
Results may differ from a plain program's by a relative error of at most 0.019.
Values may be sent and summed in bfloat16 or wider, within the bound.
No kernel may reach another device: no remote copies, remote signals or barrier semaphores. Data moves between devices by JAX's collectives and lax.ppermute only.
A program may use at most 64 MiB of HBM per device.

v0:
```python
import jax
import jax.numpy as jnp
from jax import lax
from jax.sharding import PartitionSpec as P

D = 2048
HD = 128
TOP = 4
EPS = 1e-06
NEG = -1e30


def row_positions(row_ids, half_block, n_groups):
    block_ids = row_ids // half_block
    device = block_ids // 2
    target = jnp.where(block_ids % 2 == 0, device, 2 * n_groups - 1 - device)
    return target * half_block + row_ids % half_block


def slot_tables(route_block, weight_block, experts, capacity):
    tok_here, top_here = route_block.shape
    flat_ids = route_block.reshape(tok_here * top_here)
    hit_table = (flat_ids[:, None] == jnp.arange(experts, dtype=jnp.int32)[None, :]).astype(
        jnp.int32
    )
    before = jnp.cumsum(hit_table, axis=0) - hit_table
    slot_rank = jnp.sum(before * hit_table, axis=1)
    slot_index = flat_ids * capacity + slot_rank
    slot_match = (
        jnp.arange(experts * capacity, dtype=jnp.int32)[:, None] == slot_index[None, :]
    ).astype(jnp.float32)
    slot_match = slot_match.reshape(experts * capacity, tok_here, top_here)
    dispatch = jnp.sum(slot_match, axis=2)
    combine = jnp.transpose(jnp.sum(slot_match * weight_block[None, :, :], axis=2))
    return (dispatch, combine)


def expert_ffn(token_rows, gate_matrix, up_matrix, down_matrix):
    gate_act = jnp.dot(token_rows, gate_matrix, preferred_element_type=jnp.float32)
    up_act = jnp.dot(token_rows, up_matrix, preferred_element_type=jnp.float32)
    hidden = (jax.nn.silu(gate_act) * up_act).astype(jnp.bfloat16)
    return jnp.dot(hidden, down_matrix, preferred_element_type=jnp.float32)


def exp_swap(x):
    return lax.ppermute(x, "exp", perm=[(0, 1), (1, 0)])


def exp_reduce_rows(parts):
    if lax.axis_size("exp") != 2:
        return lax.psum_scatter(
            parts.astype(jnp.bfloat16), "exp", scatter_dimension=0, tiled=True
        ).astype(jnp.float32)
    half = parts.shape[0] // 2
    first = lax.axis_index("exp") == 0
    lower = parts[:half]
    upper = parts[half:]
    mine = jnp.where(first, lower, upper)
    theirs = jnp.where(first, upper, lower)
    got = exp_swap(theirs.astype(jnp.bfloat16))
    return mine + got.astype(jnp.float32)


def exp_gather_rows(rows):
    if lax.axis_size("exp") != 2:
        return lax.all_gather(rows, "exp", axis=0, tiled=True)
    got = exp_swap(rows)
    first = lax.axis_index("exp") == 0
    return jnp.where(
        first, jnp.concatenate([rows, got], axis=0), jnp.concatenate([got, rows], axis=0)
    )


def local(
    query_states,
    key_states,
    value_states,
    residual,
    out_weight,
    norm_gain,
    gate_weight,
    up_weight,
    down_weight,
    routes,
    route_weights,
    prompt_lengths,
):
    n_ctx = lax.axis_size("ctx")
    my_ctx = lax.axis_index("ctx")
    tok_here = query_states.shape[1]
    feat_width = query_states.shape[2]
    heads_dev = feat_width // HD
    half_block = tok_here // 2
    score_scale = HD ** (-0.5)
    length = prompt_lengths[0]
    local_ids = jnp.arange(tok_here, dtype=jnp.int32)
    query_pos = row_positions(my_ctx * tok_here + local_ids, half_block, n_ctx)
    decode_pos = my_ctx * tok_here + local_ids
    query_three = query_states[0].reshape(tok_here, heads_dev, HD)
    run_max = jnp.full((heads_dev, tok_here), NEG, jnp.float32)
    kv_here = jnp.concatenate([key_states[0], value_states[0]], axis=1)
    kv_all = lax.all_gather(kv_here, "ctx", axis=0, tiled=True)
    key_two = kv_all[:, :feat_width]
    value_two = kv_all[:, feat_width:]
    row_count = key_two.shape[0]
    key_pos = row_positions(jnp.arange(row_count, dtype=jnp.int32), half_block, n_ctx)
    pick_rows = (decode_pos[:, None] == key_pos[None, :]).astype(jnp.bfloat16)
    kept_keys = jnp.dot(pick_rows, key_two, preferred_element_type=jnp.float32)
    kept_values = jnp.dot(pick_rows, value_two, preferred_element_type=jnp.float32)
    old_max = run_max
    key_heads = key_two.reshape(row_count, heads_dev, HD)
    value_heads = value_two.reshape(row_count, heads_dev, HD)
    logits = (
        jnp.einsum("qhd,khd->hqk", query_three, key_heads, preferred_element_type=jnp.float32)
        * score_scale
    )
    visible = (key_pos[None, :] <= query_pos[:, None]) & (key_pos[None, :] < length)
    logits = jnp.where(visible[None], logits, NEG)
    new_max = jnp.maximum(old_max, jnp.max(logits, axis=2))
    weights = jnp.where(visible[None], jnp.exp(logits - new_max[:, :, None]), 0.0)
    new_sum = jnp.sum(weights, axis=2)
    gained = jnp.einsum(
        "hqk,khd->hqd",
        weights.astype(jnp.bfloat16),
        value_heads,
        preferred_element_type=jnp.float32,
    )
    inner_state = (new_max, new_sum, gained)
    run_max, run_sum, run_out, kept_keys, kept_values = inner_state + (kept_keys, kept_values)
    mixed = (run_out / run_sum[:, :, None]).astype(jnp.bfloat16)
    mixed = jnp.transpose(mixed, (1, 0, 2)).reshape(tok_here, feat_width)
    out_parts = jnp.einsum(
        "tc,oc->to",
        mixed,
        lax.all_gather(out_weight, "ctx", axis=0, tiled=True),
        preferred_element_type=jnp.float32,
    )
    head_total = exp_reduce_rows(out_parts)
    stream = (residual[0].astype(jnp.float32) + head_total).astype(jnp.bfloat16)
    stream_f = stream.astype(jnp.float32)
    mean_sq = jnp.mean(stream_f * stream_f, axis=1, keepdims=True)
    normed = (stream_f * lax.rsqrt(mean_sq + EPS) * norm_gain).astype(jnp.bfloat16)
    all_normed = exp_gather_rows(normed)
    capacity = min(tok_here, 2 * max(1, 3 * tok_here * TOP // (4 * n_ctx)))
    dispatch, combine = slot_tables(routes[0], route_weights[0], n_ctx, capacity)
    send_rows = jnp.dot(
        dispatch.astype(jnp.bfloat16), all_normed, preferred_element_type=jnp.float32
    ).astype(jnp.bfloat16)
    send_rows = send_rows.reshape(n_ctx, capacity, D)
    arrived = lax.all_to_all(send_rows, "ctx", split_axis=0, concat_axis=0, tiled=True)
    slot_count = arrived.shape[1]
    flat_rows = arrived.reshape(n_ctx * slot_count, D)
    produced = expert_ffn(flat_rows, gate_weight[0], up_weight[0], down_weight[0]).reshape(
        n_ctx, slot_count, D
    )
    served = lax.all_to_all(
        produced.astype(jnp.bfloat16), "ctx", split_axis=0, concat_axis=0, tiled=True
    ).astype(produced.dtype)
    results = served.reshape(n_ctx * capacity, D)
    moe_part = jnp.dot(
        combine, results, precision=lax.Precision.HIGHEST, preferred_element_type=jnp.float32
    )
    moe_rows = exp_reduce_rows(moe_part)
    layer_out = (stream.astype(jnp.float32) + moe_rows).astype(jnp.bfloat16)
    return (
        layer_out[None],
        kept_keys.astype(jnp.bfloat16)[None],
        kept_values.astype(jnp.bfloat16)[None],
    )


def solution(mesh):
    return jax.shard_map(
        local,
        mesh=mesh,
        in_specs=(
            P("req", "ctx", "exp"),
            P("req", "ctx", "exp"),
            P("req", "ctx", "exp"),
            P("req", ("ctx", "exp"), None),
            P("ctx", "exp"),
            P(),
            P("ctx", None, "exp"),
            P("ctx", None, "exp"),
            P("ctx", "exp", None),
            P("req", "ctx", None),
            P("req", "ctx", None),
            P("req"),
        ),
        out_specs=(P("req", ("ctx", "exp"), None), P("req", "ctx", "exp"), P("req", "ctx", "exp")),
        check_vma=False,
    )
```

profile of v0, /device:TPU:0, one launch (start us, length us, event | category | flops | bytes accessed | tf_op | source)
XLA Modules:
  0.0 180.0 jit_solution(15707757264715683724)
XLA Ops:
  7.2 0.0 copy-start
  7.2 0.0 all-gather.3.cloned.1.call-start
  7.2 1.6 pad_maximum_fusion
  8.9 0.0 all-gather.3.cloned.1.call-update
  8.9 0.0 all-gather.5.cloned.1.call-start
  8.9 0.7 all-gather.5.cloned.1.call-update
  10.3 0.8 copy.47
  11.1 0.1 eq.92
  11.2 0.6 reduce-window.6
  11.8 0.9 reshape_squeeze.4
  12.7 0.1 compare_and_fusion
  12.8 22.2 %all-gather.3.cloned.1.call-done = bf16[512,1024]{1,0:T(8,128)(2,1)} async-done(((bf16[64,1024]{1,0:T(8,128)(2,1)}), bf16[512,1024]{1,0:T(8,128)(2,1)}) %all-gather.3.cloned.1.call-update) | async-done | bytes 1048592 | tf_op jit(solution)/shard_map/all_gather | solution.py:102
  35.0 1.3 fusion.71
  36.3 0.2 copy.54
  36.5 0.2 copy.55
  36.7 0.3 fusion.72
  37.1 0.2 fusion.18
  37.3 0.3 fusion.15
  37.7 0.0 copy-start.2
  37.7 0.0 copy-start.3
  37.7 27.7 %all-gather.5.cloned.1.call-done = bf16[2048,512]{1,0:T(8,128)(2,1)} async-done(((bf16[256,512]{1,0:T(8,128)(2,1)}), bf16[2048,512]{1,0:T(8,128)(2,1)}) %all-gather.5.cloned.1.call-update) | async-done | bytes 2097168 | tf_op jit(solution)/shard_map/all_gather | solution.py:135
  65.4 2.3 %fusion.38 = f32[64,2048]{1,0:T(8,128)S(1)} fusion(bf16[2048,512]{1,0:T(8,128)(2,1)} %all-gather.5.cloned.1.call-done, bf16[4,8,8,128]{3,2,1,0:T(8,128)(2,1)S(1)} %fusion.15), kind=kOutput, calls=%fused_computation.52 | convolution fusion | flops 134217728 | bytes 2686976 | tf_op jit(solution)/shard_map/tc,oc->to/dot_general | solution.py:132
  67.7 0.0 copy-start.4
  67.8 1.5 collective-permute-start
  69.3 0.2 slice_reduce_fusion
  69.5 0.1 eq.88
  69.7 0.1 fusion.48
  69.8 0.1 reduce_sum.49
  69.9 3.6 %collective-permute-done = bf16[32,2048]{1,0:T(8,128)(2,1)S(1)} collective-permute-done((bf16[32,2048]{1,0:T(8,128)(2,1)S(1)}, bf16[32,2048]{1,0:T(8,128)(2,1)S(1)}, u32[]{:S(2)}, u32[]{:S(2)}) %collective-permute-start) | collective-permute-done | bytes 131104 | tf_op jit(solution)/shard_map/ppermute | solution.py:46
  73.5 0.0 copy-done.2
  73.5 0.2 fusion.20
  73.7 0.0 copy-done.3
  73.7 0.1 fusion.22
  73.8 1.5 collective-permute-start.1
  75.3 0.1 copy.50
  75.4 0.0 copy-done.4
  75.4 0.1 convert_reduce_fusion
  75.6 3.3 %collective-permute-done.1 = bf16[32,2048]{1,0:T(8,128)(2,1)S(1)} collective-permute-done((bf16[32,2048]{1,0:T(8,128)(2,1)S(1)}, bf16[32,2048]{1,0:T(8,128)(2,1)S(1)}, u32[]{:S(2)}, u32[]{:S(2)}) %collective-permute-start.1) | collective-permute-done | bytes 131104 | tf_op jit(solution)/shard_map/ppermute | solution.py:46
  78.8 0.6 convolution_convert_fusion.1
  79.4 0.0 copy-start.5
  79.4 41.0 %all_to_all.10 = bf16[8,48,2048]{2,1,0:T(8,128)(2,1)S(1)} all-to-all(bf16[8,48,2048]{2,1,0:T(8,128)(2,1)S(1)} %bitcast.73), channel_id=1, replica_groups=mesh['req'=2,'ctx'=8,'exp'=2] {'ctx'}, dimensions={0} | all-to-all | bytes 3145728 | tf_op jit(solution)/shard_map/all_to_all | solution.py:150
  120.4 0.0 copy-done.5
  120.4 0.0 copy-start.6
  120.4 0.9 fusion.3
  121.3 0.4 copy-done.6
  121.8 0.9 fusion.10
  122.7 0.2 copy.51
  122.9 0.0 copy-done
  122.9 2.1 %convolution_convert_fusion = bf16[8,48,2048]{2,1,0:T(8,128)(2,1)} fusion(bf16[8,48,352]{2,1,0:T(8,128)(2,1)S(1)} %bitcast.77, bf16[1,352,2048]{2,1,0:T(8,128)(2,1)S(1)} %copy-done), kind=kOutput, calls=%fused_computation | convolution fusion | flops 554434560 | bytes 3284992 | tf_op jit(solution)/shard_map/dot_general | solution.py:42
  125.1 3.6 %all-to-all-start.1 = ((bf16[8,48,2048]{2,1,0:T(8,128)(2,1)}), bf16[8,48,2048]{2,1,0:T(8,128)(2,1)S(1)}, u32[]{:S(2)}, u32[]{:S(2)}) async-start(bf16[8,48,2048]{2,1,0:T(8,128)(2,1)} %convolution_convert_fusion), calls=%async_computation.1 | async-start | bytes 3145728 | tf_op jit(solution)/shard_map/all_to_all | solution.py:156
  128.7 1.9 %fusion.17 = bf16[1,64,512]{2,1,0:T(8,128)(2,1)} fusion(s32[512]{0:T(512)S(1)} %fusion.56, s32[64]{0:T(128)S(1)} %iota_add_fusion, bf16[512,1024]{1,0:T(8,128)(2,1)} %all-gather.3.cloned.1.call-done), kind=kOutput, calls=%fused_computation.19 | convolution fusion | flops 33619968 | bytes 592128 | tf_op jit(solution)/shard_map/dot_general | solution.py:109
  130.6 35.8 %all-to-all-done.1 = bf16[8,48,2048]{2,1,0:T(8,128)(2,1)S(1)} async-done(((bf16[8,48,2048]{2,1,0:T(8,128)(2,1)}), bf16[8,48,2048]{2,1,0:T(8,128)(2,1)S(1)}, u32[]{:S(2)}, u32[]{:S(2)}) %all-to-all-start.1) | async-done | bytes 1572896 | tf_op jit(solution)/shard_map/all_to_all | solution.py:156
  166.4 0.0 copy-start.1
  166.4 0.9 fusion.73
  167.3 1.5 collective-permute-start.2
  168.8 0.0 copy-done.1
  168.8 0.9 fusion.16
  169.7 2.7 %collective-permute-done.2 = bf16[32,2048]{1,0:T(8,128)(2,1)S(1)} collective-permute-done((bf16[32,2048]{1,0:T(8,128)(2,1)S(1)}, bf16[32,2048]{1,0:T(8,128)(2,1)S(1)}, u32[]{:S(2)}, u32[]{:S(2)}) %collective-permute-start.2) | collective-permute-done | bytes 131104 | tf_op jit(solution)/shard_map/ppermute | solution.py:46
  172.4 0.7 fusion.37
  (12 shorter events, 0.2 us)
Async XLA Ops:
  7.2 115.8 %copy-start = (bf16[1,352,2048]{2,1,0:T(8,128)(2,1)S(1)}, bf16[1,352,2048]{2,1,0:T(8,128)(2,1)}, u32[]{:S(2)}) copy-start(bf16[1,352,2048]{2,1,0:T(8,128)(2,1)} %param.20) | copy-start | bytes 4325380
  7.2 27.9 %all-gather.3.cloned.1.call-start = ((), (), s32[]{:S(2)}) async-start(), calls=%async_computation.2 | async-start | bytes 1179648 | tf_op jit(solution)/shard_map/all_gather | solution.py:102
  8.9 56.5 %all-gather.5.cloned.1.call-start = ((), (), s32[]{:S(2)}) async-start(), calls=%async_computation.3 | async-start | bytes 2359296 | tf_op jit(solution)/shard_map/all_gather | solution.py:135
  37.7 35.8 %copy-start.2 = (bf16[1,32,2048]{2,1,0:T(8,128)(2,1)S(1)}, bf16[1,32,2048]{2,1,0:T(8,128)(2,1)}, u32[]{:S(2)}) copy-start(bf16[1,32,2048]{2,1,0:T(8,128)(2,1)} %param.15) | copy-start | bytes 393220
  37.7 36.0 %copy-start.3 = (f32[2048]{0:T(1024)S(1)}, f32[2048]{0:T(1024)}, u32[]{:S(2)}) copy-start(f32[2048]{0:T(1024)} %param.17) | copy-start | bytes 24580
  67.7 7.7 %copy-start.4 = (f32[1,64,4]{1,2,0:T(4,128)S(1)}, f32[1,64,4]{1,2,0:T(4,128)}, u32[]{:S(2)}) copy-start(f32[1,64,4]{1,2,0:T(4,128)} %param.22) | copy-start | bytes 3076
  67.8 5.7 %collective-permute-start = (bf16[32,2048]{1,0:T(8,128)(2,1)S(1)}, bf16[32,2048]{1,0:T(8,128)(2,1)S(1)}, u32[]{:S(2)}, u32[]{:S(2)}) collective-permute-start(bf16[32,2048]{1,0:T(8,128)(2,1)S(1)} %select_convert_fusion.1), channel_id=1, source_target_pairs={{0,1},{1,0},{2,3},{3,2},{4,5},{5,4},{6,7},{7,6},{8,9},{9,8},{10,11... | collective-permute-start | bytes 393224 | tf_op jit(solution)/shard_map/ppermute | solution.py:46
  73.8 5.0 %collective-permute-start.1 = (bf16[32,2048]{1,0:T(8,128)(2,1)S(1)}, bf16[32,2048]{1,0:T(8,128)(2,1)S(1)}, u32[]{:S(2)}, u32[]{:S(2)}) collective-permute-start(bf16[32,2048]{1,0:T(8,128)(2,1)S(1)} %fusion.22), channel_id=1, source_target_pairs={{0,1},{1,0},{2,3},{3,2},{4,5},{5,4},{6,7},{7,6},{8,9},{9,8},{10,11... | collective-permute-start | bytes 393224 | tf_op jit(solution)/shard_map/ppermute | solution.py:46
  79.4 41.0 %copy-start.5 = (bf16[1,2048,352]{1,2,0:T(8,128)(2,1)S(1)}, bf16[1,2048,352]{1,2,0:T(8,128)(2,1)}, u32[]{:S(2)}) copy-start(bf16[1,2048,352]{1,2,0:T(8,128)(2,1)} %param.18) | copy-start | bytes 4325380
  120.4 1.4 copy-start.6
  125.1 41.3 %all-to-all-start.1 = ((bf16[8,48,2048]{2,1,0:T(8,128)(2,1)}), bf16[8,48,2048]{2,1,0:T(8,128)(2,1)S(1)}, u32[]{:S(2)}, u32[]{:S(2)}) async-start(bf16[8,48,2048]{2,1,0:T(8,128)(2,1)} %convolution_convert_fusion), calls=%async_computation.1 | async-start | bytes 3145728 | tf_op jit(solution)/shard_map/all_to_all | solution.py:156
  166.4 2.4 %copy-start.1 = (bf16[512,1024]{1,0:T(8,128)(2,1)S(1)}, bf16[512,1024]{1,0:T(8,128)(2,1)}, u32[]{:S(2)}) copy-start(bf16[512,1024]{1,0:T(8,128)(2,1)} %all-gather.3.cloned.1.call-done) | copy-start | bytes 3145732
  167.3 5.1 %collective-permute-start.2 = (bf16[32,2048]{1,0:T(8,128)(2,1)S(1)}, bf16[32,2048]{1,0:T(8,128)(2,1)S(1)}, u32[]{:S(2)}, u32[]{:S(2)}) collective-permute-start(bf16[32,2048]{1,0:T(8,128)(2,1)S(1)} %select_convert_fusion), channel_id=1, source_target_pairs={{0,1},{1,0},{2,3},{3,2},{4,5},{5,4},{6,7},{7,6},{8,9},{9,8},{10,11... | collective-permute-start | bytes 393224 | tf_op jit(solution)/shard_map/ppermute | solution.py:46
Sparse Core Ops, SparseCore 0:
  10.2 24.8 all-gather.2
  36.6 28.7 all-gather.4
where the time goes:
time: 180 us
  waiting for transfers between devices  96.1 us (53%)
  blocking collectives  41 us (23%)
  between operations  14.9 us (8%)
  matrix products  11.2 us (6%)
  starting transfers between devices  8.24 us (5%)
  local copies, waits for them, and re-layouts  4.62 us (3%)
  other arithmetic  3.95 us (2%)
    all_to_all x1, blocking collectives, local(): lax.all_to_all(send_rows, 'ctx', split_axis=0, concat_axis=0, tiled=True)  41 us
    all_to_all x1, waiting for transfers between devices, local(): lax.all_to_all(produced.astype(jnp.bfloat16), 'ctx', split_axis=0, concat...  35.8 us
    all_gather x1, waiting for transfers between devices, local(): lax.all_gather(out_weight, 'ctx', axis=0, tiled=True)  27.7 us
    all_gather x1, waiting for transfers between devices, local(): kv_all = lax.all_gather(kv_here, 'ctx', axis=0, tiled=True)  22.2 us
    ppermute x3, waiting for transfers between devices, exp_swap(): return lax.ppermute(x, 'exp', perm=[(0, 1), (1, 0)])  9.58 us
    ppermute x3, starting transfers between devices, exp_swap(): return lax.ppermute(x, 'exp', perm=[(0, 1), (1, 0)])  4.58 us
  transfers between devices with their start and end apart: 6, of which 6 were waited for; matrix products, arithmetic and copies ran while one was open for 5% of the time, Pallas kernels for 0%

commit v1 on v0

--- a/solution.py
+++ b/solution.py
@@ -8,6 +8,31 @@
 TOP = 4
 EPS = 1e-06
 NEG = -1e30
+
+
+def in_order(blocks, dim):
+    lengths = list(blocks.shape[1:])
+    lengths[dim] *= blocks.shape[0]
+    return jnp.moveaxis(blocks, 0, dim).reshape(lengths)
+
+
+def ring_apply(shard, axis, dim, apply, out_dim):
+    peers, place, width = (lax.axis_size(axis), lax.axis_index(axis), shard.shape[dim])
+    upward = [(i, (i + 1) % peers) for i in range(peers)]
+    backward = [(i, (i - 1) % peers) for i in range(peers)]
+    halfway = peers // 2
+    pieces = {}
+    from_left = from_right = shard
+    for hop in range(halfway + 1):
+        next_left = lax.ppermute(from_left, axis, upward) if hop < halfway else None
+        next_right = lax.ppermute(from_right, axis, backward) if hop < peers - halfway - 1 else None
+        pieces[-hop] = apply(from_left, (place - hop) % peers * width)
+        if 0 < hop < peers - halfway:
+            pieces[hop] = apply(from_right, (place + hop) % peers * width)
+        from_left, from_right = (next_left, next_right)
+    pieces = jnp.stack([pieces[k] for k in sorted(pieces)])
+    pieces = pieces[(jnp.arange(peers) - place + halfway) % peers]
+    return in_order(pieces, out_dim)
 
 
 def row_positions(row_ids, half_block, n_groups):
@@ -129,11 +154,14 @@
     run_max, run_sum, run_out, kept_keys, kept_values = inner_state + (kept_keys, kept_values)
     mixed = (run_out / run_sum[:, :, None]).astype(jnp.bfloat16)
     mixed = jnp.transpose(mixed, (1, 0, 2)).reshape(tok_here, feat_width)
-    out_parts = jnp.einsum(
-        "tc,oc->to",
-        mixed,
-        lax.all_gather(out_weight, "ctx", axis=0, tiled=True),
-        preferred_element_type=jnp.float32,
+    out_parts = ring_apply(
+        out_weight,
+        "ctx",
+        0,
+        lambda own_block, offset: jnp.einsum(
+            "tc,oc->to", mixed, own_block, preferred_element_type=jnp.float32
+        ),
+        1,
     )
     head_total = exp_reduce_rows(out_parts)
     stream = (residual[0].astype(jnp.float32) + head_total).astype(jnp.bfloat16)

time: 180 us -> 170 us (0.944)
  waiting for transfers between devices: 96.1 us -> 68.5 us
  starting transfers between devices: 8.24 us -> 20 us
  matrix products: 11.2 us -> 14.3 us
    all_gather x1 -> x0, waiting for transfers between devices: 27.7 us -> none  [local(): lax.all_gather(out_weight, 'ctx', axis=0, tiled=True)]
    ppermute x0 -> x7, waiting for transfers between devices: none -> 22.7 us  [the longest x4 21.1 us: ring_apply(): next_left = lax.ppermute(from_left, axis, upward) if hop < halfway else None]
    all_gather x1, waiting for transfers between devices: 22.2 us -> 0.02 us  [local(): kv_all = lax.all_gather(kv_here, 'ctx', axis=0, tiled=True)]
    ppermute x0 -> x7, starting transfers between devices: none -> 12.1 us  [the longest x3 11.6 us: ring_apply(): lax.ppermute(from_right, axis, backward)]
    dot_general x1 -> x8, matrix products: 2.33 us -> 5.39 us  [local(): jnp.einsum('tc,oc->to', mixed, own_block, preferred_element_type=jnp.floa...]
  transfers between devices with their start and end apart: 6 -> 12, of which waited for: 6 -> 10; matrix products, arithmetic and copies ran while one was open for 5% -> 8% of each run, Pallas kernels for 0% -> 0%
where the time goes in v1:
time: 170 us; the launch traced here: 169 us
  waiting for transfers between devices  68.5 us (40%)
  blocking collectives  42.5 us (25%)
  starting transfers between devices  20 us (12%)
  between operations  15 us (9%)
  matrix products  14.3 us (8%)
  local copies, waits for them, and re-layouts  5.25 us (3%)
  other arithmetic  3.99 us (2%)
    all_to_all x1, blocking collectives, local(): lax.all_to_all(send_rows, 'ctx', split_axis=0, concat_axis=0, tiled=True)  42.5 us
    all_to_all x1, waiting for transfers between devices, local(): lax.all_to_all(produced.astype(jnp.bfloat16), 'ctx', split_axis=0, concat...  35.8 us
    ppermute x4, waiting for transfers between devices, ring_apply(): next_left = lax.ppermute(from_left, axis, upward) if hop < halfway else None  21.1 us
    ppermute x3, starting transfers between devices, ring_apply(): lax.ppermute(from_right, axis, backward)  11.6 us
    ppermute x3, waiting for transfers between devices, exp_swap(): return lax.ppermute(x, 'exp', perm=[(0, 1), (1, 0)])  9.95 us
    dot_general x8, matrix products, local(): jnp.einsum('tc,oc->to', mixed, own_block, preferred_element_type=jnp.floa...  5.39 us
    ppermute x3, starting transfers between devices, exp_swap(): return lax.ppermute(x, 'exp', perm=[(0, 1), (1, 0)])  4.22 us
    all_to_all x1, starting transfers between devices, local(): lax.all_to_all(produced.astype(jnp.bfloat16), 'ctx', split_axis=0, concat...  3.58 us
  transfers between devices with their start and end apart: 12, of which 10 were waited for; matrix products, arithmetic and copies ran while one was open for 8% of the time, Pallas kernels for 0%

profile of v1, /device:TPU:0, one launch (start us, length us, event | category | flops | bytes accessed | tf_op | source)
XLA Modules:
  0.0 169.5 jit_solution(3915362880297165946)
XLA Ops:
  7.2 0.0 copy-start
  7.2 0.0 all-gather.2.cloned.1.call-start
  7.2 1.6 pad_maximum_fusion
  8.9 0.0 all-gather.2.cloned.1.call-update
  8.9 0.5 collective-permute-start
  9.4 4.1 %collective-permute-start.4 = (bf16[256,512]{1,0:T(8,128)(2,1)}, bf16[256,512]{1,0:T(8,128)(2,1)S(1)}, u32[]{:S(2)}, u32[]{:S(2)}) collective-permute-start(bf16[256,512]{1,0:T(8,128)(2,1)} %param.16), channel_id=1, source_target_pairs={{0,14},{2,0},{4,2},{6,4},{8,6},{10,8},{12,10},{14,12},{1,15},{3,1}... | collective-permute-start | bytes 786440 | tf_op jit(solution)/shard_map/ppermute | solution.py:28
  14.1 0.8 copy.53
  14.9 0.1 eq.94
  15.1 0.6 reduce-window.6
  15.7 0.2 slice_reduce_fusion
  15.9 2.0 %collective-permute-done = bf16[256,512]{1,0:T(8,128)(2,1)S(1)} collective-permute-done((bf16[256,512]{1,0:T(8,128)(2,1)}, bf16[256,512]{1,0:T(8,128)(2,1)S(1)}, u32[]{:S(2)}, u32[]{:S(2)}) %collective-permute-start) | collective-permute-done | bytes 262176 | tf_op jit(solution)/shard_map/ppermute | solution.py:27
  17.9 0.1 eq.90
  18.0 0.1 fusion.70
  18.1 0.3 collective-permute-done.4
  18.5 3.7 %collective-permute-start.5 = (bf16[256,512]{1,0:T(8,128)(2,1)S(1)}, bf16[256,512]{1,0:T(8,128)(2,1)}, u32[]{:S(2)}, u32[]{:S(2)}) collective-permute-start(bf16[256,512]{1,0:T(8,128)(2,1)S(1)} %collective-permute-done.4), channel_id=1, source_target_pairs={{0,14},{2,0},{4,2},{6,4},{8,6},{10,8},{12,10},{14,12},{1,15},{3,1}... | collective-permute-start | bytes 786440 | tf_op jit(solution)/shard_map/ppermute | solution.py:28
  22.2 4.6 %collective-permute-done.1 = bf16[256,512]{1,0:T(8,128)(2,1)S(1)} collective-permute-done((bf16[256,512]{1,0:T(8,128)(2,1)S(1)}, bf16[256,512]{1,0:T(8,128)(2,1)S(1)}, u32[]{:S(2)}, u32[]{:S(2)}) %collective-permute-start.1) | collective-permute-done | bytes 262176 | tf_op jit(solution)/shard_map/ppermute | solution.py:27
  26.8 0.1 reduce_sum.49
  26.9 0.9 reshape_squeeze.4
  27.7 0.1 compare_and_fusion
  27.8 1.2 collective-permute-done.5
  29.1 3.8 %collective-permute-start.6 = (bf16[256,512]{1,0:T(8,128)(2,1)}, bf16[256,512]{1,0:T(8,128)(2,1)}, u32[]{:S(2)}, u32[]{:S(2)}) collective-permute-start(bf16[256,512]{1,0:T(8,128)(2,1)} %collective-permute-done.5), channel_id=1, source_target_pairs={{0,14},{2,0},{4,2},{6,4},{8,6},{10,8},{12,10},{14,12},{1,15},{3,1}... | collective-permute-start | bytes 786440 | tf_op jit(solution)/shard_map/ppermute | solution.py:28
  32.9 6.8 %collective-permute-done.2 = bf16[256,512]{1,0:T(8,128)(2,1)} collective-permute-done((bf16[256,512]{1,0:T(8,128)(2,1)S(1)}, bf16[256,512]{1,0:T(8,128)(2,1)}, u32[]{:S(2)}, u32[]{:S(2)}) %collective-permute-start.2) | collective-permute-done | bytes 262176 | tf_op jit(solution)/shard_map/ppermute | solution.py:27
  39.7 0.0 all-gather.2.cloned.1.call-done
  39.7 1.3 fusion.95
  41.0 0.2 copy.60
  41.2 0.3 fusion.96
  41.5 0.2 copy.61
  41.7 0.2 fusion.26
  42.0 0.0 copy-start.2
  42.0 0.3 fusion.15
  42.3 7.8 %collective-permute-done.3 = bf16[256,512]{1,0:T(8,128)(2,1)} collective-permute-done((bf16[256,512]{1,0:T(8,128)(2,1)}, bf16[256,512]{1,0:T(8,128)(2,1)}, u32[]{:S(2)}, u32[]{:S(2)}) %collective-permute-start.3) | collective-permute-done | bytes 262176 | tf_op jit(solution)/shard_map/ppermute | solution.py:27
  50.1 1.2 fusion.23
  51.3 1.2 fusion.22
  52.5 0.2 fusion.21
  52.7 0.2 fusion.20
  52.9 0.2 fusion.19
  53.1 0.2 fusion.18
  53.3 1.2 fusion.17
  54.4 1.1 fusion.16
  55.6 0.6 gather_fusion
  56.2 0.0 copy-start.8
  56.3 1.1 collective-permute-start.7
  57.5 3.8 %collective-permute-done.7 = bf16[32,2048]{1,0:T(8,128)(2,1)S(1)} collective-permute-done((bf16[32,2048]{1,0:T(8,128)(2,1)S(1)}, bf16[32,2048]{1,0:T(8,128)(2,1)S(1)}, u32[]{:S(2)}, u32[]{:S(2)}) %collective-permute-start.7) | collective-permute-done | bytes 131104 | tf_op jit(solution)/shard_map/ppermute | solution.py:71
  61.3 0.2 fusion.28
  61.5 0.1 fusion.30
  61.6 1.1 collective-permute-start.8
  62.7 0.1 copy.56
  62.8 0.1 convert_reduce_fusion
  63.0 3.7 %collective-permute-done.8 = bf16[32,2048]{1,0:T(8,128)(2,1)S(1)} collective-permute-done((bf16[32,2048]{1,0:T(8,128)(2,1)S(1)}, bf16[32,2048]{1,0:T(8,128)(2,1)S(1)}, u32[]{:S(2)}, u32[]{:S(2)}) %collective-permute-start.8) | collective-permute-done | bytes 131104 | tf_op jit(solution)/shard_map/ppermute | solution.py:71
  66.6 0.6 convolution_convert_fusion.1
  67.2 42.5 %all_to_all.10 = bf16[8,48,2048]{2,1,0:T(8,128)(2,1)S(1)} all-to-all(bf16[8,48,2048]{2,1,0:T(8,128)(2,1)S(1)} %bitcast.135), channel_id=1, replica_groups=mesh['req'=2,'ctx'=8,'exp'=2] {'ctx'}, dimensions={0} | all-to-all | bytes 3145728 | tf_op jit(solution)/shard_map/all_to_all | solution.py:178
  109.7 0.9 fusion.3
  110.6 0.4 copy-done.11
  111.1 0.9 fusion.10
  112.0 0.2 copy.57
  112.2 2.2 %convolution_convert_fusion = bf16[8,48,2048]{2,1,0:T(8,128)(2,1)} fusion(bf16[8,48,352]{2,1,0:T(8,128)(2,1)S(1)} %bitcast.141, bf16[1,352,2048]{2,1,0:T(8,128)(2,1)S(1)} %copy-done), kind=kOutput, calls=%fused_computation.1 | convolution fusion | flops 554434560 | bytes 3284992 | tf_op jit(solution)/shard_map/dot_general | solution.py:67
  114.4 3.6 %all-to-all-start.1 = ((bf16[8,48,2048]{2,1,0:T(8,128)(2,1)}), bf16[8,48,2048]{2,1,0:T(8,128)(2,1)S(1)}, u32[]{:S(2)}, u32[]{:S(2)}) async-start(bf16[8,48,2048]{2,1,0:T(8,128)(2,1)} %convolution_convert_fusion), calls=%async_computation.1 | async-start | bytes 3145728 | tf_op jit(solution)/shard_map/all_to_all | solution.py:184
  118.0 1.9 %fusion.25 = bf16[1,64,512]{2,1,0:T(8,128)(2,1)} fusion(s32[512]{0:T(512)S(1)} %fusion.78, s32[64]{0:T(128)S(1)} %iota_add_fusion, bf16[512,1024]{1,0:T(8,128)(2,1)} %all-gather.2.cloned.1.call-done), kind=kOutput, calls=%fused_computation.36 | convolution fusion | flops 33619968 | bytes 592128 | tf_op jit(solution)/shard_map/dot_general | solution.py:134
  119.9 35.8 %all-to-all-done.1 = bf16[8,48,2048]{2,1,0:T(8,128)(2,1)S(1)} async-done(((bf16[8,48,2048]{2,1,0:T(8,128)(2,1)}), bf16[8,48,2048]{2,1,0:T(8,128)(2,1)S(1)}, u32[]{:S(2)}, u32[]{:S(2)}) %all-to-all-start.1) | async-done | bytes 1572896 | tf_op jit(solution)/shard_map/all_to_all | solution.py:184
  155.7 0.9 fusion.97
  156.6 2.0 %collective-permute-start.9 = (bf16[32,2048]{1,0:T(8,128)(2,1)S(1)}, bf16[32,2048]{1,0:T(8,128)(2,1)S(1)}, u32[]{:S(2)}, u32[]{:S(2)}) collective-permute-start(bf16[32,2048]{1,0:T(8,128)(2,1)S(1)} %select_convert_fusion), channel_id=1, source_target_pairs={{0,1},{1,0},{2,3},{3,2},{4,5},{5,4},{6,7},{7,6},{8,9},{9,8},{10,11... | collective-permute-start | bytes 393224 | tf_op jit(solution)/shard_map/ppermute | solution.py:71
  158.6 0.9 fusion.24
  159.5 2.4 %collective-permute-done.9 = bf16[32,2048]{1,0:T(8,128)(2,1)S(1)} collective-permute-done((bf16[32,2048]{1,0:T(8,128)(2,1)S(1)}, bf16[32,2048]{1,0:T(8,128)(2,1)S(1)}, u32[]{:S(2)}, u32[]{:S(2)}) %collective-permute-start.9) | collective-permute-done | bytes 131104 | tf_op jit(solution)/shard_map/ppermute | solution.py:71
  161.9 0.7 fusion.46
  (41 shorter events, 0.3 us)
Async XLA Ops:
  7.2 105.1 %copy-start = (bf16[1,352,2048]{2,1,0:T(8,128)(2,1)S(1)}, bf16[1,352,2048]{2,1,0:T(8,128)(2,1)}, u32[]{:S(2)}) copy-start(bf16[1,352,2048]{2,1,0:T(8,128)(2,1)} %param.20) | copy-start | bytes 4325380
  7.2 32.5 %all-gather.2.cloned.1.call-start = ((), (), s32[]{:S(2)}) async-start(), calls=%async_computation.2 | async-start | bytes 1179648 | tf_op jit(solution)/shard_map/all_gather | solution.py:127
  8.9 9.0 %collective-permute-start = (bf16[256,512]{1,0:T(8,128)(2,1)}, bf16[256,512]{1,0:T(8,128)(2,1)S(1)}, u32[]{:S(2)}, u32[]{:S(2)}) collective-permute-start(bf16[256,512]{1,0:T(8,128)(2,1)} %param.16), channel_id=1, source_target_pairs={{0,2},{2,4},{4,6},{6,8},{8,10},{10,12},{12,14},{14,0},{1,3},{3,5},... | collective-permute-start | bytes 786440 | tf_op jit(solution)/shard_map/ppermute | solution.py:27
  9.4 9.1 %collective-permute-start.4 = (bf16[256,512]{1,0:T(8,128)(2,1)}, bf16[256,512]{1,0:T(8,128)(2,1)S(1)}, u32[]{:S(2)}, u32[]{:S(2)}) collective-permute-start(bf16[256,512]{1,0:T(8,128)(2,1)} %param.16), channel_id=1, source_target_pairs={{0,14},{2,0},{4,2},{6,4},{8,6},{10,8},{12,10},{14,12},{1,15},{3,1}... | collective-permute-start | bytes 786440 | tf_op jit(solution)/shard_map/ppermute | solution.py:28
  17.9 21.8 %copy-start.3 = (bf16[256,512]{1,0:T(8,128)(2,1)}, bf16[256,512]{1,0:T(8,128)(2,1)S(1)}, u32[]{:S(2)}) copy-start(bf16[256,512]{1,0:T(8,128)(2,1)S(1)} %collective-permute-done) | copy-start | bytes 786436
  17.9 8.9 %collective-permute-start.1 = (bf16[256,512]{1,0:T(8,128)(2,1)S(1)}, bf16[256,512]{1,0:T(8,128)(2,1)S(1)}, u32[]{:S(2)}, u32[]{:S(2)}) collective-permute-start(bf16[256,512]{1,0:T(8,128)(2,1)S(1)} %collective-permute-done), channel_id=1, source_target_pairs={{0,2},{2,4},{4,6},{6,8},{8,10},{10,12},{12,14},{14,0},{1,3},{3,5},... | collective-permute-start | bytes 786440 | tf_op jit(solution)/shard_map/ppermute | solution.py:27
  18.5 10.6 %collective-permute-start.5 = (bf16[256,512]{1,0:T(8,128)(2,1)S(1)}, bf16[256,512]{1,0:T(8,128)(2,1)}, u32[]{:S(2)}, u32[]{:S(2)}) collective-permute-start(bf16[256,512]{1,0:T(8,128)(2,1)S(1)} %collective-permute-done.4), channel_id=1, source_target_pairs={{0,14},{2,0},{4,2},{6,4},{8,6},{10,8},{12,10},{14,12},{1,15},{3,1}... | collective-permute-start | bytes 786440 | tf_op jit(solution)/shard_map/ppermute | solution.py:28
  26.7 12.9 %copy-start.5 = (bf16[256,512]{1,0:T(8,128)(2,1)}, bf16[256,512]{1,0:T(8,128)(2,1)S(1)}, u32[]{:S(2)}) copy-start(bf16[256,512]{1,0:T(8,128)(2,1)S(1)} %collective-permute-done.1) | copy-start | bytes 786436
  26.7 12.9 %collective-permute-start.2 = (bf16[256,512]{1,0:T(8,128)(2,1)S(1)}, bf16[256,512]{1,0:T(8,128)(2,1)}, u32[]{:S(2)}, u32[]{:S(2)}) collective-permute-start(bf16[256,512]{1,0:T(8,128)(2,1)S(1)} %collective-permute-done.1), channel_id=1, source_target_pairs={{0,2},{2,4},{4,6},{6,8},{8,10},{10,12},{12,14},{14,0},{1,3},{3,5},... | collective-permute-start | bytes 786440 | tf_op jit(solution)/shard_map/ppermute | solution.py:27
  29.1 25.4 %collective-permute-start.6 = (bf16[256,512]{1,0:T(8,128)(2,1)}, bf16[256,512]{1,0:T(8,128)(2,1)}, u32[]{:S(2)}, u32[]{:S(2)}) collective-permute-start(bf16[256,512]{1,0:T(8,128)(2,1)} %collective-permute-done.5), channel_id=1, source_target_pairs={{0,14},{2,0},{4,2},{6,4},{8,6},{10,8},{12,10},{14,12},{1,15},{3,1}... | collective-permute-start | bytes 786440 | tf_op jit(solution)/shard_map/ppermute | solution.py:28
  39.7 10.5 %collective-permute-start.3 = (bf16[256,512]{1,0:T(8,128)(2,1)}, bf16[256,512]{1,0:T(8,128)(2,1)}, u32[]{:S(2)}, u32[]{:S(2)}) collective-permute-start(bf16[256,512]{1,0:T(8,128)(2,1)} %collective-permute-done.2), channel_id=1, source_target_pairs={{0,2},{2,4},{4,6},{6,8},{8,10},{10,12},{12,14},{14,0},{1,3},{3,5},... | collective-permute-start | bytes 786440 | tf_op jit(solution)/shard_map/ppermute | solution.py:27
  41.7 10.7 %copy-start.6 = (bf16[256,512]{1,0:T(8,128)(2,1)S(1)}, bf16[256,512]{1,0:T(8,128)(2,1)}, u32[]{:S(2)}) copy-start(bf16[256,512]{1,0:T(8,128)(2,1)} %copy-done.5) | copy-start | bytes 786436
  41.7 10.9 %copy-start.4 = (bf16[256,512]{1,0:T(8,128)(2,1)S(1)}, bf16[256,512]{1,0:T(8,128)(2,1)}, u32[]{:S(2)}) copy-start(bf16[256,512]{1,0:T(8,128)(2,1)} %copy-done.3) | copy-start | bytes 786436
  42.0 10.9 %copy-start.2 = (bf16[256,512]{1,0:T(8,128)(2,1)S(1)}, bf16[256,512]{1,0:T(8,128)(2,1)}, u32[]{:S(2)}) copy-start(bf16[256,512]{1,0:T(8,128)(2,1)} %param.16) | copy-start | bytes 786436
  55.6 5.7 %copy-start.7 = (bf16[1,32,2048]{2,1,0:T(8,128)(2,1)S(1)}, bf16[1,32,2048]{2,1,0:T(8,128)(2,1)}, u32[]{:S(2)}) copy-start(bf16[1,32,2048]{2,1,0:T(8,128)(2,1)} %param.15) | copy-start | bytes 393220
  56.2 5.3 %copy-start.8 = (f32[2048]{0:T(1024)S(1)}, f32[2048]{0:T(1024)}, u32[]{:S(2)}) copy-start(f32[2048]{0:T(1024)} %param.17) | copy-start | bytes 24580
  56.2 6.6 %copy-start.9 = (f32[1,64,4]{1,2,0:T(4,128)S(1)}, f32[1,64,4]{1,2,0:T(4,128)}, u32[]{:S(2)}) copy-start(f32[1,64,4]{1,2,0:T(4,128)} %param.22) | copy-start | bytes 3076
  56.3 5.0 %collective-permute-start.7 = (bf16[32,2048]{1,0:T(8,128)(2,1)S(1)}, bf16[32,2048]{1,0:T(8,128)(2,1)S(1)}, u32[]{:S(2)}, u32[]{:S(2)}) collective-permute-start(bf16[32,2048]{1,0:T(8,128)(2,1)S(1)} %bitcast.144), channel_id=1, source_target_pairs={{0,1},{1,0},{2,3},{3,2},{4,5},{5,4},{6,7},{7,6},{8,9},{9,8},{10,11... | collective-permute-start | bytes 393224 | tf_op jit(solution)/shard_map/ppermute | solution.py:71
  61.6 5.0 %collective-permute-start.8 = (bf16[32,2048]{1,0:T(8,128)(2,1)S(1)}, bf16[32,2048]{1,0:T(8,128)(2,1)S(1)}, u32[]{:S(2)}, u32[]{:S(2)}) collective-permute-start(bf16[32,2048]{1,0:T(8,128)(2,1)S(1)} %fusion.30), channel_id=1, source_target_pairs={{0,1},{1,0},{2,3},{3,2},{4,5},{5,4},{6,7},{7,6},{8,9},{9,8},{10,11... | collective-permute-start | bytes 393224 | tf_op jit(solution)/shard_map/ppermute | solution.py:71
  67.2 42.5 %copy-start.10 = (bf16[1,2048,352]{1,2,0:T(8,128)(2,1)S(1)}, bf16[1,2048,352]{1,2,0:T(8,128)(2,1)}, u32[]{:S(2)}) copy-start(bf16[1,2048,352]{1,2,0:T(8,128)(2,1)} %param.18) | copy-start | bytes 4325380
  109.7 1.4 copy-start.11
  114.4 41.3 %all-to-all-start.1 = ((bf16[8,48,2048]{2,1,0:T(8,128)(2,1)}), bf16[8,48,2048]{2,1,0:T(8,128)(2,1)S(1)}, u32[]{:S(2)}, u32[]{:S(2)}) async-start(bf16[8,48,2048]{2,1,0:T(8,128)(2,1)} %convolution_convert_fusion), calls=%async_computation.1 | async-start | bytes 3145728 | tf_op jit(solution)/shard_map/all_to_all | solution.py:184
  155.7 2.9 %copy-start.1 = (bf16[512,1024]{1,0:T(8,128)(2,1)S(1)}, bf16[512,1024]{1,0:T(8,128)(2,1)}, u32[]{:S(2)}) copy-start(bf16[512,1024]{1,0:T(8,128)(2,1)} %all-gather.2.cloned.1.call-done) | copy-start | bytes 3145732
  156.6 5.3 %collective-permute-start.9 = (bf16[32,2048]{1,0:T(8,128)(2,1)S(1)}, bf16[32,2048]{1,0:T(8,128)(2,1)S(1)}, u32[]{:S(2)}, u32[]{:S(2)}) collective-permute-start(bf16[32,2048]{1,0:T(8,128)(2,1)S(1)} %select_convert_fusion), channel_id=1, source_target_pairs={{0,1},{1,0},{2,3},{3,2},{4,5},{5,4},{6,7},{7,6},{8,9},{9,8},{10,11... | collective-permute-start | bytes 393224 | tf_op jit(solution)/shard_map/ppermute | solution.py:71
Sparse Core Ops, SparseCore 0:
  10.2 29.0 all-gather.1
